TPU v7x, 128 devices: a whole 4x4x4 slice. The times are simulated.
128 devices in a mesh: gx: 16 (over z, y), gy: 8 (over x, core).
Axes of the slice: x: 4, y: 4, z: 4, core: 2. Of those that a mesh axis runs over, the one named last changes fastest.
Arguments:
- tile_sums: bfloat16 [16384, 5, 16384], P(('gx', 'gy')), may hold values from -180 to 180
- tile_dest: int32 [16384], P(('gx', 'gy')), may hold values from 0 to 127, as said below
- tile_place: int32 [16384], P(('gx', 'gy')), may hold values from 0 to 15
- tile_count: int32 [128], P(('gx', 'gy')), may hold values from 64 to 128, as said below
Outputs:
- smoothed: float32 [5, 16, 1024, 2048], P(None, 'gx', 'gy')
Inputs may be any that keep to these rules, and one draw needn't show every extreme that they name: `tile_dest`: each DEM device's 128 records name every filter device exactly once. Only the first tile_count[d] slots of device d are live; some device has all 128 live and some has half.
All inputs are finite; a program needn't handle non-finite values.
Results may differ from a plain program's by a relative error of at most 0.0003.
Values may be sent and summed in bfloat16 or wider, within the bound.
No kernel may reach another device: no remote copies, remote signals or barrier semaphores. Data moves between devices by JAX's collectives and lax.ppermute only.
A program may use at most 192 MiB of HBM per device.

v0:
```python
import math

import jax
import jax.numpy as jnp
from jax import lax
from jax.sharding import PartitionSpec as P

TE = 32
BX = 4
BY = 4
RADIUS = 4


def padded_2(cells, sides, width):
    for axis, dim in sides:
        count = lax.axis_size(axis)
        ends = count - 1
        head = lax.slice_in_dim(cells, 0, width, axis=dim)
        tail = lax.slice_in_dim(cells, cells.shape[dim] - width, cells.shape[dim], axis=dim)
        cells = jnp.concatenate(
            [
                lax.ppermute(tail, axis, [(i, (i + 1) % count) for i in range(ends)]),
                cells,
                lax.ppermute(head, axis, [((i + 1) % count, i) for i in range(ends)]),
            ],
            axis=dim,
        )
    return cells


def gauss_taps():
    spread = RADIUS * 5.0 / 16.0
    raw_taps = [
        math.exp(-(offset * offset) / (2.0 * spread * spread))
        for offset in range(-RADIUS, RADIUS + 1)
    ]
    total_weight = sum(raw_taps)
    return [value / total_weight for value in raw_taps]


def zero_pad(field, axis):
    widths = [(0, 0)] * field.ndim
    widths[axis] = (RADIUS, RADIUS)
    return jnp.pad(field, widths)


def smooth_axis(padded, axis, taps, length):
    result = taps[0] * lax.slice_in_dim(padded, 0, length, axis=axis)
    for offset in range(1, len(taps)):
        result = result + taps[offset] * lax.slice_in_dim(
            padded, offset, offset + length, axis=axis
        )
    return result


def local(tile_sums, tile_dest, tile_place, tile_count):
    slot_count = tile_sums.shape[0]
    fields = tile_sums.shape[1]
    cells = tile_sums.shape[2]
    planes = cells // (TE * TE)
    across = lax.axis_size("gx")
    column_count = lax.axis_size("gy")
    peer_count = across * column_count
    is_live = jnp.arange(slot_count, dtype=jnp.int32) < tile_count[0]
    targets = jnp.arange(peer_count, dtype=jnp.int32)
    chosen = (tile_dest[None, :] == targets[:, None]) & is_live[None, :]
    outgoing = jnp.dot(
        chosen.astype(jnp.bfloat16),
        tile_sums.reshape(slot_count, fields * cells),
        preferred_element_type=jnp.float32,
    ).astype(jnp.bfloat16)
    out_place = jnp.sum(jnp.where(chosen, tile_place[None, :] + 1, 0), axis=1) - 1
    incoming, in_place = (
        lax.all_to_all(outgoing, ("gx", "gy"), split_axis=0, concat_axis=0, tiled=True),
        lax.all_to_all(out_place[:, None], ("gx", "gy"), split_axis=0, concat_axis=0, tiled=True),
    )
    in_place = in_place.reshape(peer_count)
    local_ids = jnp.arange(BX * BY, dtype=jnp.int32)
    landing = (in_place[None, :] == local_ids[:, None]).astype(jnp.bfloat16)
    deposited = jnp.dot(landing, incoming, preferred_element_type=jnp.float32)
    deposited = deposited.reshape(BY, BX, fields, planes, TE, TE).transpose(2, 3, 0, 4, 1, 5)
    deposited = deposited.reshape(fields, planes, BY * TE, BX * TE)
    taps = gauss_taps()
    height = BY * TE
    width = BX * TE
    padded = padded_2(deposited, (("gx", 3), ("gy", 2)), RADIUS)
    along_x = smooth_axis(padded, 3, taps, width)
    along_y = smooth_axis(along_x, 2, taps, height)
    along_z = smooth_axis(zero_pad(along_y, 1), 1, taps, planes)
    return lax.all_to_all(along_z, "gx", split_axis=1, concat_axis=3, tiled=True)


def solution(mesh):
    return jax.shard_map(
        local,
        mesh=mesh,
        in_specs=(P(("gx", "gy"), None, None), P(("gx", "gy")), P(("gx", "gy")), P(("gx", "gy"))),
        out_specs=P(None, "gx", "gy", None),
        check_vma=False,
    )
```

profile of v0, /device:TPU:4, one launch (start us, length us, event | category | flops | bytes accessed | tf_op | source)
XLA Modules:
  0.0 865.0 jit_solution(1218308976395293217)
XLA Ops:
  2.9 10.5 %all-to-all-start = ((s32[128,1,1]{2,1,0:T(1,128)}), s32[128,1,1]{2,1,0:T(1,128)S(1)}, u32[]{:S(2)}, u32[]{:S(2)}) async-start(s32[128,1,1]{2,1,0:T(1,128)} %copy.38), calls=%async_computation | async-start | bytes 131072 | tf_op jit(solution)/shard_map/all_to_all | solution.py:75
  13.4 27.3 %copy.39 = bf16[128,5,16384]{0,2,1:T(8,128)(2,1)} copy(bf16[128,5,16384]{2,0,1:T(8,128)(2,1)} %param.4) | data formatting | bytes 41943040 | tf_op args[0]
  40.7 17.5 %fusion = bf16[128,1,81920]{2,0,1:T(8,128)(2,1)} fusion(bf16[128,81920]{0,1:T(8,128)(2,1)} %bitcast.30, s32[128]{0:T(128)S(1)} %copy-done.2, pred[128]{0:T(512)(128)(4,1)S(1)} %iota_compare_fusion.1), kind=kOutput, calls=%fused_computation.1 | convolution fusion | flops 2694873088 | bytes 41943680 | tf_op jit(solution)/shard_map/dot_general | solution.py:67
  58.7 23.9 %reduce.1 = bf16[128,81920]{1,0:T(8,128)(2,1)} reduce(bf16[128,1,81920]{2,0,1:T(8,128)(2,1)} %fusion, bf16[]{:T(256)} %broadcast.93), dimensions={1}, to_apply=%copy.40.reduce_sub_computation | reduce | bytes 41943040 | tf_op jit(solution)/shard_map/all_to_all | solution.py:74
  82.6 25.6 %reshape.54 = bf16[128,2,40960]{2,1,0:T(2,128)(2,1)} reshape(bf16[128,81920]{1,0:T(8,128)(2,1)} %reduce.1) | data formatting | bytes 41943040
  108.2 10.2 %all-to-all-start.1 = ((bf16[128,2,40960]{2,1,0:T(2,128)(2,1)}), bf16[128,2,40960]{2,1,0:T(2,128)(2,1)}, u32[]{:S(2)}, u32[]{:S(2)}) async-start(bf16[128,2,40960]{2,1,0:T(2,128)(2,1)} %reshape.54), calls=%async_computation.1 | async-start | bytes 41943040 | tf_op jit(solution)/shard_map/all_to_all | solution.py:74
  120.8 295.7 %all-to-all-done.1 = bf16[128,2,40960]{2,1,0:T(2,128)(2,1)} async-done(((bf16[128,2,40960]{2,1,0:T(2,128)(2,1)}), bf16[128,2,40960]{2,1,0:T(2,128)(2,1)}, u32[]{:S(2)}, u32[]{:S(2)}) %all-to-all-start.1) | async-done | bytes 20971552 | tf_op jit(solution)/shard_map/all_to_all | solution.py:74
  416.4 78.9 %reshape.55 = bf16[128,1,81920]{2,1,0:T(2,128)(2,1)} reshape(bf16[128,2,40960]{2,1,0:T(2,128)(2,1)} %all-to-all-done.1) | data formatting | bytes 41943040
  495.3 80.1 %copy.41 = bf16[128,1,81920]{0,2,1:T(8,128)(2,1)} copy(bf16[128,1,81920]{2,1,0:T(2,128)(2,1)} %reshape.55) | data formatting | bytes 41943040 | tf_op jit(solution)/shard_map/all_to_all | solution.py:74
  575.5 34.0 %convolution_bitcast_fusion = f32[5,16,4,32,4,32]{5,4,3,1,0,2:T(4,128)} fusion(bf16[5,16,32,32,128,1]{4,3,2,1,0,5:T(8,128)(2,1)} %bitcast.31, s32[4,4]{1,0:T(4,128)S(1)} %multiply_add_fusion, s32[128]{0:T(128)S(1)} %reduce), kind=kOutput, calls=%fused_computation.11 | convolution fusion | flops 335546368 | bytes 26214976 | tf_op jit(solution)/shard_map/dot_general | solution.py:80
  609.5 17.5 %copy.42 = f32[5,16,4,32,4,32]{5,4,3,2,1,0:T(4,128)} copy(f32[5,16,4,32,4,32]{5,4,3,1,0,2:T(4,128)} %convolution_bitcast_fusion) | data formatting | bytes 10485760 | tf_op jit(solution)/shard_map/transpose | solution.py:81
  626.9 16.5 %reshape.50 = f32[5,16,128,128]{3,2,1,0:T(8,128)} reshape(f32[5,16,4,32,4,32]{5,4,3,2,1,0:T(4,128)} %copy.42) | data formatting | bytes 10485760 | tf_op jit(solution)/shard_map/reshape | solution.py:82
  643.4 9.6 %fusion.41 = (f32[5,16,128,4]{3,2,1,0:T(8,128)}, f32[5,16,128,4]{3,2,1,0:T(8,128)}) fusion(f32[5,16,128,128]{3,2,1,0:T(8,128)} %reshape.50), kind=kLoop, calls=%fused_computation.78 | loop fusion | bytes 655360 | tf_op jit(solution)/shard_map/slice | solution.py:19
  656.3 4.6 collective-permute-start
  661.0 3.3 copy.44
  668.8 10.2 %collective-permute-done.1 = f32[5,16,128,4]{2,1,3,0:T(8,128)S(1)} collective-permute-done((f32[5,16,128,4]{2,1,3,0:T(8,128)S(1)}, f32[5,16,128,4]{2,1,3,0:T(8,128)S(1)}, u32[]{:S(2)}, u32[]{:S(2)}) %collective-permute-start.1) | collective-permute-done | bytes 163872 | tf_op jit(solution)/shard_map/ppermute | solution.py:24
  686.5 3.5 collective-permute-start.3
  694.6 11.4 %pad_maximum_fusion = f32[5,16,136,136]{3,2,1,0:T(8,128)} fusion(f32[5,16,4,136]{3,2,1,0:T(4,128)S(1)} %collective-permute-done.3, f32[5,16,128,4]{3,2,1,0:T(8,128)S(1)} %copy-done.1, f32[5,16,128,128]{3,2,1,0:T(8,128)S(1)} %bitcast.29, f32[5,16,128,4]{3,2,1,0:T(8,128)S(1)} %copy-done, f32[5,16,4,136]{3,2,1,0:T(4,128)S(1)} %collective-permute-done.2), kind=kLoop, calls=%fused_computation.10 | loop fusion | flops 5918720 | bytes 11837440 | tf_op jit(solution)/shard_map/concatenate | solution.py:20
  706.0 34.0 %fusion.1 = f32[5,16,136,128]{3,2,1,0:T(8,128)} fusion(f32[5,16,136,136]{3,2,1,0:T(8,128)} %pad_maximum_fusion), kind=kLoop, calls=%fused_computation.13 | loop fusion | flops 23674880 | bytes 55705600 | tf_op jit(solution)/shard_map/add | solution.py:50
  740.0 20.8 %fusion.25 = f32[5,16,128,128]{3,2,1,0:T(8,128)} fusion(f32[5,16,136,128]{3,2,1,0:T(8,128)} %fusion.1), kind=kLoop, calls=%fused_computation.46 | loop fusion | flops 22282240 | bytes 52428800 | tf_op jit(solution)/shard_map/add | solution.py:50
  760.8 16.6 %fusion.17 = f32[5,16,128,128]{3,2,1,0:T(8,128)S(1)} fusion(f32[5,16,128,128]{3,2,1,0:T(8,128)} %fusion.25), kind=kLoop, calls=%fused_computation.37 | loop fusion | flops 22282240 | bytes 10485760 | tf_op jit(solution)/shard_map/add | solution.py:50
  777.8 75.3 %all_to_all.36 = f32[5,16,128,128]{3,2,0,1:T(8,128)} all-to-all(f32[5,16,128,128]{3,2,0,1:T(8,128)S(1)} %copy.47), channel_id=1, replica_groups=mesh['gx'=16,'gy'=8] {'gx'}, dimensions={1} | all-to-all | bytes 10485760 | tf_op jit(solution)/shard_map/all_to_all | solution.py:90
  853.2 5.9 copy.48
  859.1 5.9 copy.49
  (30 shorter events, 25.3 us)
Async XLA Ops:
  2.9 105.4 %all-to-all-start = ((s32[128,1,1]{2,1,0:T(1,128)}), s32[128,1,1]{2,1,0:T(1,128)S(1)}, u32[]{:S(2)}, u32[]{:S(2)}) async-start(s32[128,1,1]{2,1,0:T(1,128)} %copy.38), calls=%async_computation | async-start | bytes 131072 | tf_op jit(solution)/shard_map/all_to_all | solution.py:75
  13.4 27.3 %copy-start.2 = (s32[128]{0:T(128)S(1)}, s32[128]{0:T(128)}, u32[]{:S(2)}) copy-start(s32[128]{0:T(128)} %param.5) | copy-start | bytes 1540
  108.2 308.2 %all-to-all-start.1 = ((bf16[128,2,40960]{2,1,0:T(2,128)(2,1)}), bf16[128,2,40960]{2,1,0:T(2,128)(2,1)}, u32[]{:S(2)}, u32[]{:S(2)}) async-start(bf16[128,2,40960]{2,1,0:T(2,128)(2,1)} %reshape.54), calls=%async_computation.1 | async-start | bytes 41943040 | tf_op jit(solution)/shard_map/all_to_all | solution.py:74
  656.3 9.2 %collective-permute-start = (f32[5,16,128,4]{2,1,3,0:T(8,128)S(1)}, f32[5,16,128,4]{2,1,3,0:T(8,128)S(1)}, u32[]{:S(2)}, u32[]{:S(2)}) collective-permute-start(f32[5,16,128,4]{2,1,3,0:T(8,128)S(1)} %copy.43), channel_id=1, source_target_pairs={{0,8},{8,16},{16,24},{24,32},{32,40},{40,48},{48,56},{56,64},{64,7... | collective-permute-start | bytes 491528 | tf_op jit(solution)/shard_map/ppermute | solution.py:22
  664.3 14.6 %collective-permute-start.1 = (f32[5,16,128,4]{2,1,3,0:T(8,128)S(1)}, f32[5,16,128,4]{2,1,3,0:T(8,128)S(1)}, u32[]{:S(2)}, u32[]{:S(2)}) collective-permute-start(f32[5,16,128,4]{2,1,3,0:T(8,128)S(1)} %copy.44), channel_id=1, source_target_pairs={{8,0},{16,8},{24,16},{32,24},{40,32},{48,40},{56,48},{64,56},{72,6... | collective-permute-start | bytes 491528 | tf_op jit(solution)/shard_map/ppermute | solution.py:24
  678.9 15.7 %slice-start = ((s8[5242880]{0:T(1024)(128)(4,1)}), s8[1048576]{0:T(1024)(128)(4,1)S(1)}, s32[]{:S(2)}) async-start(s8[5242880]{0:T(1024)(128)(4,1)} %bitcast.28), calls=%async_computation.3 | async-start | bytes 2097152
  682.0 12.6 %slice-start.1 = ((s8[5242880]{0:T(1024)(128)(4,1)}), s8[4194304]{0:T(1024)(128)(4,1)S(1)}, s32[]{:S(2)}) async-start(s8[5242880]{0:T(1024)(128)(4,1)} %bitcast.28), calls=%async_computation.4 | async-start | bytes 8388608
  682.0 12.6 %copy-start = (f32[5,16,128,4]{3,2,1,0:T(8,128)S(1)}, f32[5,16,128,4]{3,2,1,0:T(8,128)}, u32[]{:S(2)}) copy-start(f32[5,16,128,4]{3,2,1,0:T(8,128)} %copy.45) | copy-start | bytes 491524
  682.0 12.6 %copy-start.1 = (f32[5,16,128,4]{3,2,1,0:T(8,128)S(1)}, f32[5,16,128,4]{3,2,1,0:T(8,128)}, u32[]{:S(2)}) copy-start(f32[5,16,128,4]{3,2,1,0:T(8,128)} %copy.46) | copy-start | bytes 491524
  684.2 8.7 %collective-permute-start.2 = (f32[5,16,4,136]{3,2,1,0:T(4,128)S(1)}, f32[5,16,4,136]{3,2,1,0:T(4,128)S(1)}, u32[]{:S(2)}, u32[]{:S(2)}) collective-permute-start(f32[5,16,4,136]{3,2,1,0:T(4,128)S(1)} %get-tuple-element.5), channel_id=1, source_target_pairs={{0,1},{1,2},{2,3},{3,4},{4,5},{5,6},{6,7},{8,9},{9,10},{10,11},{11... | collective-permute-start | bytes 522248 | tf_op jit(solution)/shard_map/ppermute | solution.py:22
  686.5 8.1 collective-permute-start.3
where the time goes:
time: 871 us; the launch traced here: 865 us
  waiting for transfers between devices  310 us (36%)
  local copies, waits for them, and re-layouts  282 us (32%)
  other arithmetic  113 us (13%)
  blocking collectives  75.3 us (9%)
  matrix products  51.6 us (6%)
  starting transfers between devices  32.4 us (4%)
    all_to_all x1, waiting for transfers between devices, local(): lax.all_to_all(outgoing, ('gx', 'gy'), split_axis=0, concat_axis=0, tiled...  296 us
    unnamed x13, local copies, waits for them, and re-layouts  132 us
    all_to_all x2, local copies, waits for them, and re-layouts, local(): lax.all_to_all(outgoing, ('gx', 'gy'), split_axis=0, concat_axis=0, tiled...  80.6 us
    all_to_all x1, blocking collectives, local(): lax.all_to_all(along_z, 'gx', split_axis=1, concat_axis=3, tiled=True)  75.3 us
    add x3, other arithmetic, smooth_axis(): result + taps[offset] * lax.slice_in_dim(padded, offset, offset + length,...  71.5 us
    dot_general x1, matrix products, local(): deposited = jnp.dot(landing, incoming, preferred_element_type=jnp.float32)  34 us
    all_to_all x1, other arithmetic, local(): lax.all_to_all(outgoing, ('gx', 'gy'), split_axis=0, concat_axis=0, tiled...  23.9 us
    dot_general x1, matrix products, local(): jnp.dot(chosen.astype(jnp.bfloat16), tile_sums.reshape(slot_count, fields...  17.5 us
  transfers between devices with their start and end apart: 6, of which 4 were waited for; matrix products, arithmetic and copies ran while one was open for 12% of the time, Pallas kernels for 0%

commit v1 on v0

v1 whole, which is shorter than its diff:
```python
import math

import jax
import jax.numpy as jnp
import numpy as np
from jax import lax
from jax.sharding import PartitionSpec as P

TE = 32
BX = 4
BY = 4
RADIUS = 4
HIGHEST = lax.Precision.HIGHEST


def gauss_taps():
    spread = RADIUS * 5.0 / 16.0
    raw_taps = [
        math.exp(-(offset * offset) / (2.0 * spread * spread))
        for offset in range(-RADIUS, RADIUS + 1)
    ]
    total_weight = sum(raw_taps)
    return [value / total_weight for value in raw_taps]


def band(length_in, length_out, shift):
    taps = gauss_taps()
    mat = np.zeros((length_in, length_out), np.float32)
    for j in range(length_out):
        for k in range(2 * RADIUS + 1):
            i = j + shift + k - RADIUS
            if 0 <= i < length_in:
                mat[i, j] = taps[k]
    return jnp.asarray(mat)


def halo(cells, axis, dim, width):
    count = lax.axis_size(axis)
    ends = count - 1
    head = lax.slice_in_dim(cells, 0, width, axis=dim)
    tail = lax.slice_in_dim(cells, cells.shape[dim] - width, cells.shape[dim], axis=dim)
    return jnp.concatenate(
        [
            lax.ppermute(tail, axis, [(i, (i + 1) % count) for i in range(ends)]),
            cells,
            lax.ppermute(head, axis, [((i + 1) % count, i) for i in range(ends)]),
        ],
        axis=dim,
    )


def local(tile_sums, tile_dest, tile_place, tile_count):
    slot_count, fields, cells = tile_sums.shape
    planes = cells // (TE * TE)
    across = lax.axis_size("gx")
    column_count = lax.axis_size("gy")
    peer_count = across * column_count
    is_live = jnp.arange(slot_count, dtype=jnp.int32) < tile_count[0]
    targets = jnp.arange(peer_count, dtype=jnp.int32)
    chosen = tile_dest[None, :] == targets[:, None]
    pick = chosen.astype(jnp.bfloat16)
    out_place = jnp.sum(jnp.where(chosen & is_live[None, :], tile_place[None, :] + 1, 0), axis=1) - 1
    in_place = lax.all_to_all(out_place[:, None], ("gx", "gy"), 0, 0, tiled=True).reshape(peer_count)
    local_ids = jnp.arange(BX * BY, dtype=jnp.int32)
    landing = (in_place[None, :] == local_ids[:, None]).astype(jnp.bfloat16)
    height = BY * TE
    width = BX * TE
    wz = band(planes, planes, 0)
    wx = band(width + 2 * RADIUS, width, RADIUS)
    wy = band(height + 2 * RADIUS, height, RADIUS)
    rows = cells // 128
    outs = []
    for f in range(fields):
        record = tile_sums[:, f, :]
        outgoing = jnp.dot(pick, record, preferred_element_type=jnp.float32).astype(jnp.bfloat16)
        outgoing = outgoing.reshape(peer_count, rows, 128)
        incoming = lax.all_to_all(outgoing, ("gx", "gy"), 0, 0, tiled=True)
        deposited = jnp.einsum("ts,src->trc", landing, incoming, preferred_element_type=jnp.float32)
        deposited = deposited.reshape(BY, BX, planes, TE, TE).transpose(2, 0, 3, 1, 4)
        deposited = deposited.reshape(planes, height, width)
        along_z = jnp.einsum("io,iyx->oyx", wz, deposited, precision=HIGHEST)
        padded = halo(along_z, "gx", 2, RADIUS)
        along_x = jnp.einsum("zyi,ix->zyx", padded, wx, precision=HIGHEST)
        padded = halo(along_x, "gy", 1, RADIUS)
        along_y = jnp.einsum("iy,zix->zyx", wy, padded, precision=HIGHEST)
        outs.append(lax.all_to_all(along_y, "gx", 0, 2, tiled=True))
    return jnp.stack(outs, axis=0)


def solution(mesh):
    return jax.shard_map(
        local,
        mesh=mesh,
        in_specs=(P(("gx", "gy"), None, None), P(("gx", "gy")), P(("gx", "gy")), P(("gx", "gy"))),
        out_specs=P(None, "gx", "gy", None),
        check_vma=False,
    )
```

time: 871 us -> 594 us (0.68)
  local copies, waits for them, and re-layouts: 282 us -> 139 us
  waiting for transfers between devices: 310 us -> 192 us
  starting transfers between devices: 32.4 us -> 148 us
  other arithmetic: 113 us -> 17.4 us
  blocking collectives: 75.3 us -> 0 us
  matrix products: 51.6 us -> 85 us
    unnamed x13 -> x29, local copies, waits for them, and re-layouts: 132 us -> 25 us
    all_to_all x2 -> x11, waiting for transfers between devices: 296 us -> 190 us  [the longest x5 176 us: local(): incoming = lax.all_to_all(outgoing, ('gx', 'gy'), 0, 0, tiled=True)]
    all_to_all x4 -> x0, local copies, waits for them, and re-layouts: 92.4 us -> none  [the longest x2 80.6 us: local(): lax.all_to_all(outgoing, ('gx', 'gy'), split_axis=0, concat_axis=0, tiled...]
    all_to_all x1 -> x0, blocking collectives: 75.3 us -> none  [local(): lax.all_to_all(along_z, 'gx', split_axis=1, concat_axis=3, tiled=True)]
    add x3 -> x0, other arithmetic: 71.5 us -> none  [smooth_axis(): result + taps[offset] * lax.slice_in_dim(padded, offset, offset + length,...]
    all_to_all x2 -> x11, starting transfers between devices: 20.7 us -> 91.2 us  [the longest x5 41.3 us: local(): outs.append(lax.all_to_all(along_y, 'gx', 0, 2, tiled=True))]
    reshape x1 -> x15, local copies, waits for them, and re-layouts: 16.5 us -> 68.9 us  [the longest x10 55 us: local(): deposited = deposited.reshape(planes, height, width)]
    ppermute x4 -> x20, starting transfers between devices: 11.7 us -> 56.5 us  [the longest x10 30.8 us: halo(): lax.ppermute(tail, axis, [(i, (i + 1) % count) for i in range(ends)])]
  transfers between devices with their start and end apart: 6 -> 31, of which waited for: 4 -> 8; matrix products, arithmetic and copies ran while one was open for 12% -> 40% of each run, Pallas kernels for 0% -> 0%
where the time goes in v1:
time: 594 us; the launch traced here: 582 us
  waiting for transfers between devices  192 us (32%)
  starting transfers between devices  148 us (25%)
  local copies, waits for them, and re-layouts  139 us (23%)
  matrix products  85 us (14%)
  other arithmetic  17.4 us (3%)
    all_to_all x5, waiting for transfers between devices, local(): incoming = lax.all_to_all(outgoing, ('gx', 'gy'), 0, 0, tiled=True)  176 us
    reshape x10, local copies, waits for them, and re-layouts, local(): deposited = deposited.reshape(planes, height, width)  55 us
    all_to_all x5, starting transfers between devices, local(): outs.append(lax.all_to_all(along_y, 'gx', 0, 2, tiled=True))  41.3 us
    all_to_all x5, starting transfers between devices, local(): incoming = lax.all_to_all(outgoing, ('gx', 'gy'), 0, 0, tiled=True)  39.4 us
    ppermute x10, starting transfers between devices, halo(): lax.ppermute(tail, axis, [(i, (i + 1) % count) for i in range(ends)])  30.8 us
    ppermute x10, starting transfers between devices, halo(): lax.ppermute(head, axis, [((i + 1) % count, i) for i in range(ends)])  25.7 us
    unnamed x29, local copies, waits for them, and re-layouts  25 us
    dot_general x5, matrix products, local(): along_y = jnp.einsum('iy,zix->zyx', wy, padded, precision=HIGHEST)  23.4 us
  transfers between devices with their start and end apart: 31, of which 8 were waited for; matrix products, arithmetic and copies ran while one was open for 40% of the time, Pallas kernels for 0%

profile of v1, /device:TPU:4, one launch (start us, length us, event | category | flops | bytes accessed | tf_op | source)
XLA Modules:
  0.0 582.4 jit_solution(6314442446567608436)
XLA Ops:
  2.9 10.5 %all-to-all-start = ((s32[128,1,1]{2,1,0:T(1,128)}), s32[128,1,1]{2,1,0:T(1,128)S(1)}, u32[]{:S(2)}, u32[]{:S(2)}) async-start(s32[128,1,1]{2,1,0:T(1,128)} %copy.175), calls=%async_computation | async-start | bytes 131072 | tf_op jit(solution)/shard_map/all_to_all | solution.py:63
  21.3 8.9 %all-to-all-start.3 = ((bf16[128,128,128]{2,1,0:T(8,128)(2,1)}), bf16[128,128,128]{2,1,0:T(8,128)(2,1)}, u32[]{:S(2)}, u32[]{:S(2)}) async-start(bf16[128,128,128]{2,1,0:T(8,128)(2,1)} %bitcast.129), calls=%async_computation.3 | async-start | bytes 8388608 | tf_op jit(solution)/shard_map/all_to_all | solution.py:77
  37.0 43.9 %all-to-all-done.3 = bf16[128,128,128]{2,1,0:T(8,128)(2,1)} async-done(((bf16[128,128,128]{2,1,0:T(8,128)(2,1)}), bf16[128,128,128]{2,1,0:T(8,128)(2,1)}, u32[]{:S(2)}, u32[]{:S(2)}) %all-to-all-start.3) | async-done | bytes 4194336 | tf_op jit(solution)/shard_map/all_to_all | solution.py:77
  80.9 7.5 %all-to-all-start.1 = ((bf16[128,128,128]{2,1,0:T(8,128)(2,1)}), bf16[128,128,128]{2,1,0:T(8,128)(2,1)}, u32[]{:S(2)}, u32[]{:S(2)}) async-start(bf16[128,128,128]{2,1,0:T(8,128)(2,1)} %bitcast.130), calls=%async_computation.1 | async-start | bytes 8388608 | tf_op jit(solution)/shard_map/all_to_all | solution.py:77
  95.1 44.1 %all-to-all-done.1 = bf16[128,128,128]{2,1,0:T(8,128)(2,1)} async-done(((bf16[128,128,128]{2,1,0:T(8,128)(2,1)}), bf16[128,128,128]{2,1,0:T(8,128)(2,1)}, u32[]{:S(2)}, u32[]{:S(2)}) %all-to-all-start.1) | async-done | bytes 4194336 | tf_op jit(solution)/shard_map/all_to_all | solution.py:77
  139.1 7.5 %all-to-all-start.5 = ((bf16[128,128,128]{2,1,0:T(8,128)(2,1)}), bf16[128,128,128]{2,1,0:T(8,128)(2,1)}, u32[]{:S(2)}, u32[]{:S(2)}) async-start(bf16[128,128,128]{2,1,0:T(8,128)(2,1)} %bitcast.131), calls=%async_computation.5 | async-start | bytes 8388608 | tf_op jit(solution)/shard_map/all_to_all | solution.py:77
  153.3 44.0 %all-to-all-done.5 = bf16[128,128,128]{2,1,0:T(8,128)(2,1)} async-done(((bf16[128,128,128]{2,1,0:T(8,128)(2,1)}), bf16[128,128,128]{2,1,0:T(8,128)(2,1)}, u32[]{:S(2)}, u32[]{:S(2)}) %all-to-all-start.5) | async-done | bytes 4194336 | tf_op jit(solution)/shard_map/all_to_all | solution.py:77
  197.4 7.9 %all-to-all-start.7 = ((bf16[128,128,128]{2,1,0:T(8,128)(2,1)}), bf16[128,128,128]{2,1,0:T(8,128)(2,1)}, u32[]{:S(2)}, u32[]{:S(2)}) async-start(bf16[128,128,128]{2,1,0:T(8,128)(2,1)} %bitcast.132), calls=%async_computation.7 | async-start | bytes 8388608 | tf_op jit(solution)/shard_map/all_to_all | solution.py:77
  212.0 43.8 %all-to-all-done.7 = bf16[128,128,128]{2,1,0:T(8,128)(2,1)} async-done(((bf16[128,128,128]{2,1,0:T(8,128)(2,1)}), bf16[128,128,128]{2,1,0:T(8,128)(2,1)}, u32[]{:S(2)}, u32[]{:S(2)}) %all-to-all-start.7) | async-done | bytes 4194336 | tf_op jit(solution)/shard_map/all_to_all | solution.py:77
  255.8 7.5 %all-to-all-start.9 = ((bf16[128,128,128]{2,1,0:T(8,128)(2,1)}), bf16[128,128,128]{2,1,0:T(8,128)(2,1)}, u32[]{:S(2)}, u32[]{:S(2)}) async-start(bf16[128,128,128]{2,1,0:T(8,128)(2,1)} %bitcast.128), calls=%async_computation.9 | async-start | bytes 8388608 | tf_op jit(solution)/shard_map/all_to_all | solution.py:77
  273.1 6.9 %copy.227 = f32[16,4,32,4,32]{4,3,0,2,1:T(4,128)} copy(f32[16,4,32,4,32]{4,2,0,3,1:T(8,128)} %bitcast.123) | data formatting | bytes 2097152 | tf_op jit(solution)/shard_map/reshape | solution.py:80
  298.4 6.9 %copy.226 = f32[16,4,32,4,32]{4,3,0,2,1:T(4,128)} copy(f32[16,4,32,4,32]{4,2,0,3,1:T(8,128)} %bitcast.124) | data formatting | bytes 2097152 | tf_op jit(solution)/shard_map/reshape | solution.py:80
  311.8 4.5 collective-permute-start
  325.6 6.8 %copy.228 = f32[16,4,32,4,32]{4,3,0,2,1:T(4,128)} copy(f32[16,4,32,4,32]{4,2,0,3,1:T(8,128)} %bitcast.125) | data formatting | bytes 2097152 | tf_op jit(solution)/shard_map/reshape | solution.py:80
  351.0 7.0 %copy.229 = f32[16,4,32,4,32]{4,3,0,2,1:T(4,128)} copy(f32[16,4,32,4,32]{4,2,0,3,1:T(8,128)} %bitcast.126) | data formatting | bytes 2097152 | tf_op jit(solution)/shard_map/reshape | solution.py:80
  358.0 4.5 reshape.92
  375.9 6.9 %copy.230 = f32[16,4,32,4,32]{4,3,0,2,1:T(4,128)} copy(f32[16,4,32,4,32]{4,2,0,3,1:T(8,128)} %bitcast.127) | data formatting | bytes 2097152 | tf_op jit(solution)/shard_map/reshape | solution.py:80
  382.8 4.9 reshape.93
  418.9 5.7 convolution_bitcast_fusion.3
  424.5 14.5 %all-to-all-start.4 = ((f32[16,128,128]{1,2,0:T(8,128)}), f32[16,128,128]{1,2,0:T(8,128)}, u32[]{:S(2)}, u32[]{:S(2)}) async-start(f32[16,128,128]{1,2,0:T(8,128)} %convolution_bitcast_fusion.3), calls=%async_computation.4 | async-start | bytes 2097152 | tf_op jit(solution)/shard_map/all_to_all | solution.py:86
  463.2 7.2 %all-to-all-start.2 = ((f32[16,128,128]{1,2,0:T(8,128)}), f32[16,128,128]{1,2,0:T(8,128)}, u32[]{:S(2)}, u32[]{:S(2)}) async-start(f32[16,128,128]{1,2,0:T(8,128)} %convolution_bitcast_fusion.4), calls=%async_computation.2 | async-start | bytes 2097152 | tf_op jit(solution)/shard_map/all_to_all | solution.py:86
  498.6 8.0 %all-to-all-start.6 = ((f32[16,128,128]{1,2,0:T(8,128)}), f32[16,128,128]{1,2,0:T(8,128)}, u32[]{:S(2)}, u32[]{:S(2)}) async-start(f32[16,128,128]{1,2,0:T(8,128)} %convolution_bitcast_fusion.2), calls=%async_computation.6 | async-start | bytes 2097152 | tf_op jit(solution)/shard_map/all_to_all | solution.py:86
  524.1 7.2 %all-to-all-start.8 = ((f32[16,128,128]{1,2,0:T(8,128)}), f32[16,128,128]{1,2,0:T(8,128)S(1)}, u32[]{:S(2)}, u32[]{:S(2)}) async-start(f32[16,128,128]{1,2,0:T(8,128)} %convolution_bitcast_fusion.1), calls=%async_computation.8 | async-start | bytes 2097152 | tf_op jit(solution)/shard_map/all_to_all | solution.py:86
  565.4 10.0 %all-to-all-done.10 = f32[16,128,128]{1,2,0:T(8,128)S(1)} async-done(((f32[16,128,128]{1,2,0:T(8,128)}), f32[16,128,128]{1,2,0:T(8,128)S(1)}, u32[]{:S(2)}, u32[]{:S(2)}) %all-to-all-start.10) | async-done | bytes 1048608 | tf_op jit(solution)/shard_map/all_to_all | solution.py:86
  (159 shorter events, 254.3 us)
Async XLA Ops:
  2.9 18.5 %all-to-all-start = ((s32[128,1,1]{2,1,0:T(1,128)}), s32[128,1,1]{2,1,0:T(1,128)S(1)}, u32[]{:S(2)}, u32[]{:S(2)}) async-start(s32[128,1,1]{2,1,0:T(1,128)} %copy.175), calls=%async_computation | async-start | bytes 131072 | tf_op jit(solution)/shard_map/all_to_all | solution.py:63
  21.3 59.5 %all-to-all-start.3 = ((bf16[128,128,128]{2,1,0:T(8,128)(2,1)}), bf16[128,128,128]{2,1,0:T(8,128)(2,1)}, u32[]{:S(2)}, u32[]{:S(2)}) async-start(bf16[128,128,128]{2,1,0:T(8,128)(2,1)} %bitcast.129), calls=%async_computation.3 | async-start | bytes 8388608 | tf_op jit(solution)/shard_map/all_to_all | solution.py:77
  80.9 58.3 %all-to-all-start.1 = ((bf16[128,128,128]{2,1,0:T(8,128)(2,1)}), bf16[128,128,128]{2,1,0:T(8,128)(2,1)}, u32[]{:S(2)}, u32[]{:S(2)}) async-start(bf16[128,128,128]{2,1,0:T(8,128)(2,1)} %bitcast.130), calls=%async_computation.1 | async-start | bytes 8388608 | tf_op jit(solution)/shard_map/all_to_all | solution.py:77
  139.1 58.2 %all-to-all-start.5 = ((bf16[128,128,128]{2,1,0:T(8,128)(2,1)}), bf16[128,128,128]{2,1,0:T(8,128)(2,1)}, u32[]{:S(2)}, u32[]{:S(2)}) async-start(bf16[128,128,128]{2,1,0:T(8,128)(2,1)} %bitcast.131), calls=%async_computation.5 | async-start | bytes 8388608 | tf_op jit(solution)/shard_map/all_to_all | solution.py:77
  197.4 58.5 %all-to-all-start.7 = ((bf16[128,128,128]{2,1,0:T(8,128)(2,1)}), bf16[128,128,128]{2,1,0:T(8,128)(2,1)}, u32[]{:S(2)}, u32[]{:S(2)}) async-start(bf16[128,128,128]{2,1,0:T(8,128)(2,1)} %bitcast.132), calls=%async_computation.7 | async-start | bytes 8388608 | tf_op jit(solution)/shard_map/all_to_all | solution.py:77
  255.8 108.9 %all-to-all-start.9 = ((bf16[128,128,128]{2,1,0:T(8,128)(2,1)}), bf16[128,128,128]{2,1,0:T(8,128)(2,1)}, u32[]{:S(2)}, u32[]{:S(2)}) async-start(bf16[128,128,128]{2,1,0:T(8,128)(2,1)} %bitcast.128), calls=%async_computation.9 | async-start | bytes 8388608 | tf_op jit(solution)/shard_map/all_to_all | solution.py:77
  285.5 102.2 %collective-permute-start.4 = (f32[16,128,4]{1,0,2:T(8,128)S(1)}, f32[16,128,4]{1,0,2:T(8,128)S(1)}, u32[]{:S(2)}, u32[]{:S(2)}) collective-permute-start(f32[16,128,4]{1,0,2:T(8,128)S(1)} %copy.189), channel_id=1, source_target_pairs={{0,8},{8,16},{16,24},{24,32},{32,40},{40,48},{48,56},{56,64},{64,7... | collective-permute-start | bytes 98312 | tf_op jit(solution)/shard_map/ppermute | solution.py:44
  289.4 99.7 %collective-permute-start.5 = (f32[16,128,4]{1,0,2:T(8,128)S(1)}, f32[16,128,4]{1,0,2:T(8,128)S(1)}, u32[]{:S(2)}, u32[]{:S(2)}) collective-permute-start(f32[16,128,4]{1,0,2:T(8,128)S(1)} %copy.190), channel_id=1, source_target_pairs={{8,0},{16,8},{24,16},{32,24},{40,32},{48,40},{56,48},{64,56},{72,6... | collective-permute-start | bytes 98312 | tf_op jit(solution)/shard_map/ppermute | solution.py:46
  311.8 96.9 %collective-permute-start = (f32[16,128,4]{1,0,2:T(8,128)S(1)}, f32[16,128,4]{1,0,2:T(8,128)S(1)}, u32[]{:S(2)}, u32[]{:S(2)}) collective-permute-start(f32[16,128,4]{1,0,2:T(8,128)S(1)} %copy.180), channel_id=1, source_target_pairs={{0,8},{8,16},{16,24},{24,32},{32,40},{40,48},{48,56},{56,64},{64,7... | collective-permute-start | bytes 98312 | tf_op jit(solution)/shard_map/ppermute | solution.py:44
  316.8 94.6 %collective-permute-start.1 = (f32[16,128,4]{1,0,2:T(8,128)S(1)}, f32[16,128,4]{1,0,2:T(8,128)S(1)}, u32[]{:S(2)}, u32[]{:S(2)}) collective-permute-start(f32[16,128,4]{1,0,2:T(8,128)S(1)} %copy.181), channel_id=1, source_target_pairs={{8,0},{16,8},{24,16},{32,24},{40,32},{48,40},{56,48},{64,56},{72,6... | collective-permute-start | bytes 98312 | tf_op jit(solution)/shard_map/ppermute | solution.py:46
  338.9 109.2 %collective-permute-start.8 = (f32[16,128,4]{1,0,2:T(8,128)S(1)}, f32[16,128,4]{1,0,2:T(8,128)S(1)}, u32[]{:S(2)}, u32[]{:S(2)}) collective-permute-start(f32[16,128,4]{1,0,2:T(8,128)S(1)} %copy.198), channel_id=1, source_target_pairs={{0,8},{8,16},{16,24},{24,32},{32,40},{40,48},{48,56},{56,64},{64,7... | collective-permute-start | bytes 98312 | tf_op jit(solution)/shard_map/ppermute | solution.py:44
  396.6 20.8 %collective-permute-start.6 = (f32[16,4,128]{2,1,0:T(4,128)}, f32[16,4,128]{2,1,0:T(4,128)S(1)}, u32[]{:S(2)}, u32[]{:S(2)}) collective-permute-start(f32[16,4,128]{2,1,0:T(4,128)} %get-tuple-element.17), channel_id=1, source_target_pairs={{0,1},{1,2},{2,3},{3,4},{4,5},{5,6},{6,7},{8,9},{9,10},{10,11},{11... | collective-permute-start | bytes 98312 | tf_op jit(solution)/shard_map/ppermute | solution.py:44
  398.5 20.3 %collective-permute-start.7 = (f32[16,4,128]{2,1,0:T(4,128)}, f32[16,4,128]{2,1,0:T(4,128)S(1)}, u32[]{:S(2)}, u32[]{:S(2)}) collective-permute-start(f32[16,4,128]{2,1,0:T(4,128)} %get-tuple-element.18), channel_id=1, source_target_pairs={{1,0},{2,1},{3,2},{4,3},{5,4},{6,5},{7,6},{9,8},{10,9},{11,10},{12... | collective-permute-start | bytes 98312 | tf_op jit(solution)/shard_map/ppermute | solution.py:46
  408.7 44.7 %collective-permute-start.9 = (f32[16,128,4]{1,0,2:T(8,128)}, f32[16,128,4]{1,0,2:T(8,128)S(1)}, u32[]{:S(2)}, u32[]{:S(2)}) collective-permute-start(f32[16,128,4]{1,0,2:T(8,128)} %copy.199), channel_id=1, source_target_pairs={{8,0},{16,8},{24,16},{32,24},{40,32},{48,40},{56,48},{64,56},{72,6... | collective-permute-start | bytes 98312 | tf_op jit(solution)/shard_map/ppermute | solution.py:46
  411.4 78.2 %collective-permute-start.12 = (f32[16,128,4]{1,0,2:T(8,128)S(1)}, f32[16,128,4]{1,0,2:T(8,128)S(1)}, u32[]{:S(2)}, u32[]{:S(2)}) collective-permute-start(f32[16,128,4]{1,0,2:T(8,128)S(1)} %copy.207), channel_id=1, source_target_pairs={{0,8},{8,16},{16,24},{24,32},{32,40},{40,48},{48,56},{56,64},{64,7... | collective-permute-start | bytes 98312 | tf_op jit(solution)/shard_map/ppermute | solution.py:44
  417.4 75.4 %collective-permute-start.13 = (f32[16,128,4]{1,0,2:T(8,128)S(1)}, f32[16,128,4]{1,0,2:T(8,128)S(1)}, u32[]{:S(2)}, u32[]{:S(2)}) collective-permute-start(f32[16,128,4]{1,0,2:T(8,128)S(1)} %copy.208), channel_id=1, source_target_pairs={{8,0},{16,8},{24,16},{32,24},{40,32},{48,40},{56,48},{64,56},{72,6... | collective-permute-start | bytes 98312 | tf_op jit(solution)/shard_map/ppermute | solution.py:46
  424.5 38.6 %all-to-all-start.4 = ((f32[16,128,128]{1,2,0:T(8,128)}), f32[16,128,128]{1,2,0:T(8,128)}, u32[]{:S(2)}, u32[]{:S(2)}) async-start(f32[16,128,128]{1,2,0:T(8,128)} %convolution_bitcast_fusion.3), calls=%async_computation.4 | async-start | bytes 2097152 | tf_op jit(solution)/shard_map/all_to_all | solution.py:86
  463.2 35.4 %all-to-all-start.2 = ((f32[16,128,128]{1,2,0:T(8,128)}), f32[16,128,128]{1,2,0:T(8,128)}, u32[]{:S(2)}, u32[]{:S(2)}) async-start(f32[16,128,128]{1,2,0:T(8,128)} %convolution_bitcast_fusion.4), calls=%async_computation.2 | async-start | bytes 2097152 | tf_op jit(solution)/shard_map/all_to_all | solution.py:86
  475.4 18.8 %collective-permute-start.10 = (f32[16,4,128]{2,1,0:T(4,128)}, f32[16,4,128]{2,1,0:T(4,128)S(1)}, u32[]{:S(2)}, u32[]{:S(2)}) collective-permute-start(f32[16,4,128]{2,1,0:T(4,128)} %get-tuple-element.13), channel_id=1, source_target_pairs={{0,1},{1,2},{2,3},{3,4},{4,5},{5,6},{6,7},{8,9},{9,10},{10,11},{11... | collective-permute-start | bytes 98312 | tf_op jit(solution)/shard_map/ppermute | solution.py:44
  484.2 33.4 %collective-permute-start.16 = (f32[16,128,4]{1,0,2:T(8,128)S(1)}, f32[16,128,4]{1,0,2:T(8,128)S(1)}, u32[]{:S(2)}, u32[]{:S(2)}) collective-permute-start(f32[16,128,4]{1,0,2:T(8,128)S(1)} %copy.216), channel_id=1, source_target_pairs={{0,8},{8,16},{16,24},{24,32},{32,40},{40,48},{48,56},{56,64},{64,7... | collective-permute-start | bytes 98312 | tf_op jit(solution)/shard_map/ppermute | solution.py:44
  489.6 28.6 %collective-permute-start.17 = (f32[16,128,4]{1,0,2:T(8,128)S(1)}, f32[16,128,4]{1,0,2:T(8,128)S(1)}, u32[]{:S(2)}, u32[]{:S(2)}) collective-permute-start(f32[16,128,4]{1,0,2:T(8,128)S(1)} %copy.217), channel_id=1, source_target_pairs={{8,0},{16,8},{24,16},{32,24},{40,32},{48,40},{56,48},{64,56},{72,6... | collective-permute-start | bytes 98312 | tf_op jit(solution)/shard_map/ppermute | solution.py:46
  498.6 25.5 %all-to-all-start.6 = ((f32[16,128,128]{1,2,0:T(8,128)}), f32[16,128,128]{1,2,0:T(8,128)}, u32[]{:S(2)}, u32[]{:S(2)}) async-start(f32[16,128,128]{1,2,0:T(8,128)} %convolution_bitcast_fusion.2), calls=%async_computation.6 | async-start | bytes 2097152 | tf_op jit(solution)/shard_map/all_to_all | solution.py:86
  524.1 26.6 %all-to-all-start.8 = ((f32[16,128,128]{1,2,0:T(8,128)}), f32[16,128,128]{1,2,0:T(8,128)S(1)}, u32[]{:S(2)}, u32[]{:S(2)}) async-start(f32[16,128,128]{1,2,0:T(8,128)} %convolution_bitcast_fusion.1), calls=%async_computation.8 | async-start | bytes 2097152 | tf_op jit(solution)/shard_map/all_to_all | solution.py:86
  550.7 24.8 %all-to-all-start.10 = ((f32[16,128,128]{1,2,0:T(8,128)}), f32[16,128,128]{1,2,0:T(8,128)S(1)}, u32[]{:S(2)}, u32[]{:S(2)}) async-start(f32[16,128,128]{1,2,0:T(8,128)} %convolution_bitcast_fusion), calls=%async_computation.10 | async-start | bytes 2097152 | tf_op jit(solution)/shard_map/all_to_all | solution.py:86
  (17 other events, 123.5 us)

commit v2 on v1

--- a/solution.py
+++ b/solution.py
@@ -69,12 +69,14 @@
     wx = band(width + 2 * RADIUS, width, RADIUS)
     wy = band(height + 2 * RADIUS, height, RADIUS)
     rows = cells // 128
-    outs = []
-    for f in range(fields):
+
+    def send(f):
         record = tile_sums[:, f, :]
         outgoing = jnp.dot(pick, record, preferred_element_type=jnp.float32).astype(jnp.bfloat16)
         outgoing = outgoing.reshape(peer_count, rows, 128)
-        incoming = lax.all_to_all(outgoing, ("gx", "gy"), 0, 0, tiled=True)
+        return lax.all_to_all(outgoing, ("gx", "gy"), 0, 0, tiled=True)
+
+    def proc(incoming):
         deposited = jnp.einsum("ts,src->trc", landing, incoming, preferred_element_type=jnp.float32)
         deposited = deposited.reshape(BY, BX, planes, TE, TE).transpose(2, 0, 3, 1, 4)
         deposited = deposited.reshape(planes, height, width)
@@ -83,7 +85,17 @@
         along_x = jnp.einsum("zyi,ix->zyx", padded, wx, precision=HIGHEST)
         padded = halo(along_x, "gy", 1, RADIUS)
         along_y = jnp.einsum("iy,zix->zyx", wy, padded, precision=HIGHEST)
-        outs.append(lax.all_to_all(along_y, "gx", 0, 2, tiled=True))
+        return lax.all_to_all(along_y, "gx", 0, 2, tiled=True)
+
+    outs = []
+    incoming = send(0)
+    for f in range(fields):
+        if f + 1 < fields:
+            following = send(f + 1)
+            outs.append(proc(incoming))
+            incoming = following
+        else:
+            outs.append(proc(incoming))
     return jnp.stack(outs, axis=0)
 
 

time: 594 us -> 594 us (level)
  no operation moved by 1% of the time
where the time goes in v2:
time: 594 us; the launch traced here: 583 us
  waiting for transfers between devices  191 us (32%)
  starting transfers between devices  148 us (25%)
  local copies, waits for them, and re-layouts  139 us (23%)
  matrix products  85 us (14%)
  other arithmetic  17.4 us (3%)
    all_to_all x5, waiting for transfers between devices, send(): return lax.all_to_all(outgoing, ('gx', 'gy'), 0, 0, tiled=True)  176 us
    reshape x10, local copies, waits for them, and re-layouts, proc(): deposited = deposited.reshape(planes, height, width)  54.8 us
    all_to_all x5, starting transfers between devices, proc(): return lax.all_to_all(along_y, 'gx', 0, 2, tiled=True)  41.6 us
    all_to_all x5, starting transfers between devices, send(): return lax.all_to_all(outgoing, ('gx', 'gy'), 0, 0, tiled=True)  39.4 us
    ppermute x10, starting transfers between devices, halo(): lax.ppermute(tail, axis, [(i, (i + 1) % count) for i in range(ends)])  30.7 us
    ppermute x10, starting transfers between devices, halo(): lax.ppermute(head, axis, [((i + 1) % count, i) for i in range(ends)])  25.9 us
    unnamed x29, local copies, waits for them, and re-layouts  25 us
    dot_general x5, matrix products, proc(): along_y = jnp.einsum('iy,zix->zyx', wy, padded, precision=HIGHEST)  23.4 us
  transfers between devices with their start and end apart: 31, of which 8 were waited for; matrix products, arithmetic and copies ran while one was open for 40% of the time, Pallas kernels for 0%

profile of v2, /device:TPU:4, one launch (start us, length us, event | category | flops | bytes accessed | tf_op | source)
XLA Modules:
  0.0 582.5 jit_solution(6314442446567608436)
XLA Ops:
  2.9 10.5 %all-to-all-start = ((s32[128,1,1]{2,1,0:T(1,128)}), s32[128,1,1]{2,1,0:T(1,128)S(1)}, u32[]{:S(2)}, u32[]{:S(2)}) async-start(s32[128,1,1]{2,1,0:T(1,128)} %copy.175), calls=%async_computation | async-start | bytes 131072 | tf_op jit(solution)/shard_map/all_to_all | solution.py:63
  21.3 8.9 %all-to-all-start.3 = ((bf16[128,128,128]{2,1,0:T(8,128)(2,1)}), bf16[128,128,128]{2,1,0:T(8,128)(2,1)}, u32[]{:S(2)}, u32[]{:S(2)}) async-start(bf16[128,128,128]{2,1,0:T(8,128)(2,1)} %bitcast.129), calls=%async_computation.3 | async-start | bytes 8388608 | tf_op jit(solution)/shard_map/all_to_all | solution.py:77
  37.0 43.9 %all-to-all-done.3 = bf16[128,128,128]{2,1,0:T(8,128)(2,1)} async-done(((bf16[128,128,128]{2,1,0:T(8,128)(2,1)}), bf16[128,128,128]{2,1,0:T(8,128)(2,1)}, u32[]{:S(2)}, u32[]{:S(2)}) %all-to-all-start.3) | async-done | bytes 4194336 | tf_op jit(solution)/shard_map/all_to_all | solution.py:77
  80.9 7.5 %all-to-all-start.1 = ((bf16[128,128,128]{2,1,0:T(8,128)(2,1)}), bf16[128,128,128]{2,1,0:T(8,128)(2,1)}, u32[]{:S(2)}, u32[]{:S(2)}) async-start(bf16[128,128,128]{2,1,0:T(8,128)(2,1)} %bitcast.130), calls=%async_computation.1 | async-start | bytes 8388608 | tf_op jit(solution)/shard_map/all_to_all | solution.py:77
  95.1 44.0 %all-to-all-done.1 = bf16[128,128,128]{2,1,0:T(8,128)(2,1)} async-done(((bf16[128,128,128]{2,1,0:T(8,128)(2,1)}), bf16[128,128,128]{2,1,0:T(8,128)(2,1)}, u32[]{:S(2)}, u32[]{:S(2)}) %all-to-all-start.1) | async-done | bytes 4194336 | tf_op jit(solution)/shard_map/all_to_all | solution.py:77
  139.1 7.5 %all-to-all-start.5 = ((bf16[128,128,128]{2,1,0:T(8,128)(2,1)}), bf16[128,128,128]{2,1,0:T(8,128)(2,1)}, u32[]{:S(2)}, u32[]{:S(2)}) async-start(bf16[128,128,128]{2,1,0:T(8,128)(2,1)} %bitcast.131), calls=%async_computation.5 | async-start | bytes 8388608 | tf_op jit(solution)/shard_map/all_to_all | solution.py:77
  153.3 44.0 %all-to-all-done.5 = bf16[128,128,128]{2,1,0:T(8,128)(2,1)} async-done(((bf16[128,128,128]{2,1,0:T(8,128)(2,1)}), bf16[128,128,128]{2,1,0:T(8,128)(2,1)}, u32[]{:S(2)}, u32[]{:S(2)}) %all-to-all-start.5) | async-done | bytes 4194336 | tf_op jit(solution)/shard_map/all_to_all | solution.py:77
  197.4 7.9 %all-to-all-start.7 = ((bf16[128,128,128]{2,1,0:T(8,128)(2,1)}), bf16[128,128,128]{2,1,0:T(8,128)(2,1)}, u32[]{:S(2)}, u32[]{:S(2)}) async-start(bf16[128,128,128]{2,1,0:T(8,128)(2,1)} %bitcast.132), calls=%async_computation.7 | async-start | bytes 8388608 | tf_op jit(solution)/shard_map/all_to_all | solution.py:77
  211.9 43.8 %all-to-all-done.7 = bf16[128,128,128]{2,1,0:T(8,128)(2,1)} async-done(((bf16[128,128,128]{2,1,0:T(8,128)(2,1)}), bf16[128,128,128]{2,1,0:T(8,128)(2,1)}, u32[]{:S(2)}, u32[]{:S(2)}) %all-to-all-start.7) | async-done | bytes 4194336 | tf_op jit(solution)/shard_map/all_to_all | solution.py:77
  255.8 7.5 %all-to-all-start.9 = ((bf16[128,128,128]{2,1,0:T(8,128)(2,1)}), bf16[128,128,128]{2,1,0:T(8,128)(2,1)}, u32[]{:S(2)}, u32[]{:S(2)}) async-start(bf16[128,128,128]{2,1,0:T(8,128)(2,1)} %bitcast.128), calls=%async_computation.9 | async-start | bytes 8388608 | tf_op jit(solution)/shard_map/all_to_all | solution.py:77
  273.0 6.9 %copy.227 = f32[16,4,32,4,32]{4,3,0,2,1:T(4,128)} copy(f32[16,4,32,4,32]{4,2,0,3,1:T(8,128)} %bitcast.123) | data formatting | bytes 2097152 | tf_op jit(solution)/shard_map/reshape | solution.py:82
  298.2 6.9 %copy.226 = f32[16,4,32,4,32]{4,3,0,2,1:T(4,128)} copy(f32[16,4,32,4,32]{4,2,0,3,1:T(8,128)} %bitcast.124) | data formatting | bytes 2097152 | tf_op jit(solution)/shard_map/reshape | solution.py:82
  311.6 4.5 collective-permute-start
  325.6 6.8 %copy.228 = f32[16,4,32,4,32]{4,3,0,2,1:T(4,128)} copy(f32[16,4,32,4,32]{4,2,0,3,1:T(8,128)} %bitcast.125) | data formatting | bytes 2097152 | tf_op jit(solution)/shard_map/reshape | solution.py:82
  351.0 7.0 %copy.229 = f32[16,4,32,4,32]{4,3,0,2,1:T(4,128)} copy(f32[16,4,32,4,32]{4,2,0,3,1:T(8,128)} %bitcast.126) | data formatting | bytes 2097152 | tf_op jit(solution)/shard_map/reshape | solution.py:82
  375.8 6.9 %copy.230 = f32[16,4,32,4,32]{4,3,0,2,1:T(4,128)} copy(f32[16,4,32,4,32]{4,2,0,3,1:T(8,128)} %bitcast.127) | data formatting | bytes 2097152 | tf_op jit(solution)/shard_map/reshape | solution.py:82
  382.7 4.7 reshape.93
  418.9 5.7 convolution_bitcast_fusion.3
  424.5 14.5 %all-to-all-start.4 = ((f32[16,128,128]{1,2,0:T(8,128)}), f32[16,128,128]{1,2,0:T(8,128)}, u32[]{:S(2)}, u32[]{:S(2)}) async-start(f32[16,128,128]{1,2,0:T(8,128)} %convolution_bitcast_fusion.3), calls=%async_computation.4 | async-start | bytes 2097152 | tf_op jit(solution)/shard_map/all_to_all | solution.py:88
  463.1 7.2 %all-to-all-start.2 = ((f32[16,128,128]{1,2,0:T(8,128)}), f32[16,128,128]{1,2,0:T(8,128)}, u32[]{:S(2)}, u32[]{:S(2)}) async-start(f32[16,128,128]{1,2,0:T(8,128)} %convolution_bitcast_fusion.4), calls=%async_computation.2 | async-start | bytes 2097152 | tf_op jit(solution)/shard_map/all_to_all | solution.py:88
  498.4 8.0 %all-to-all-start.6 = ((f32[16,128,128]{1,2,0:T(8,128)}), f32[16,128,128]{1,2,0:T(8,128)}, u32[]{:S(2)}, u32[]{:S(2)}) async-start(f32[16,128,128]{1,2,0:T(8,128)} %convolution_bitcast_fusion.2), calls=%async_computation.6 | async-start | bytes 2097152 | tf_op jit(solution)/shard_map/all_to_all | solution.py:88
  523.9 7.2 %all-to-all-start.8 = ((f32[16,128,128]{1,2,0:T(8,128)}), f32[16,128,128]{1,2,0:T(8,128)S(1)}, u32[]{:S(2)}, u32[]{:S(2)}) async-start(f32[16,128,128]{1,2,0:T(8,128)} %convolution_bitcast_fusion.1), calls=%async_computation.8 | async-start | bytes 2097152 | tf_op jit(solution)/shard_map/all_to_all | solution.py:88
  550.2 4.7 all-to-all-start.10
  565.3 10.0 %all-to-all-done.10 = f32[16,128,128]{1,2,0:T(8,128)S(1)} async-done(((f32[16,128,128]{1,2,0:T(8,128)}), f32[16,128,128]{1,2,0:T(8,128)S(1)}, u32[]{:S(2)}, u32[]{:S(2)}) %all-to-all-start.10) | async-done | bytes 1048608 | tf_op jit(solution)/shard_map/all_to_all | solution.py:88
  (159 shorter events, 254.2 us)
Async XLA Ops:
  2.9 18.5 %all-to-all-start = ((s32[128,1,1]{2,1,0:T(1,128)}), s32[128,1,1]{2,1,0:T(1,128)S(1)}, u32[]{:S(2)}, u32[]{:S(2)}) async-start(s32[128,1,1]{2,1,0:T(1,128)} %copy.175), calls=%async_computation | async-start | bytes 131072 | tf_op jit(solution)/shard_map/all_to_all | solution.py:63
  21.3 59.5 %all-to-all-start.3 = ((bf16[128,128,128]{2,1,0:T(8,128)(2,1)}), bf16[128,128,128]{2,1,0:T(8,128)(2,1)}, u32[]{:S(2)}, u32[]{:S(2)}) async-start(bf16[128,128,128]{2,1,0:T(8,128)(2,1)} %bitcast.129), calls=%async_computation.3 | async-start | bytes 8388608 | tf_op jit(solution)/shard_map/all_to_all | solution.py:77
  80.9 58.3 %all-to-all-start.1 = ((bf16[128,128,128]{2,1,0:T(8,128)(2,1)}), bf16[128,128,128]{2,1,0:T(8,128)(2,1)}, u32[]{:S(2)}, u32[]{:S(2)}) async-start(bf16[128,128,128]{2,1,0:T(8,128)(2,1)} %bitcast.130), calls=%async_computation.1 | async-start | bytes 8388608 | tf_op jit(solution)/shard_map/all_to_all | solution.py:77
  139.1 58.2 %all-to-all-start.5 = ((bf16[128,128,128]{2,1,0:T(8,128)(2,1)}), bf16[128,128,128]{2,1,0:T(8,128)(2,1)}, u32[]{:S(2)}, u32[]{:S(2)}) async-start(bf16[128,128,128]{2,1,0:T(8,128)(2,1)} %bitcast.131), calls=%async_computation.5 | async-start | bytes 8388608 | tf_op jit(solution)/shard_map/all_to_all | solution.py:77
  197.4 58.4 %all-to-all-start.7 = ((bf16[128,128,128]{2,1,0:T(8,128)(2,1)}), bf16[128,128,128]{2,1,0:T(8,128)(2,1)}, u32[]{:S(2)}, u32[]{:S(2)}) async-start(bf16[128,128,128]{2,1,0:T(8,128)(2,1)} %bitcast.132), calls=%async_computation.7 | async-start | bytes 8388608 | tf_op jit(solution)/shard_map/all_to_all | solution.py:77
  255.8 108.9 %all-to-all-start.9 = ((bf16[128,128,128]{2,1,0:T(8,128)(2,1)}), bf16[128,128,128]{2,1,0:T(8,128)(2,1)}, u32[]{:S(2)}, u32[]{:S(2)}) async-start(bf16[128,128,128]{2,1,0:T(8,128)(2,1)} %bitcast.128), calls=%async_computation.9 | async-start | bytes 8388608 | tf_op jit(solution)/shard_map/all_to_all | solution.py:77
  285.5 102.0 %collective-permute-start.4 = (f32[16,128,4]{1,0,2:T(8,128)S(1)}, f32[16,128,4]{1,0,2:T(8,128)S(1)}, u32[]{:S(2)}, u32[]{:S(2)}) collective-permute-start(f32[16,128,4]{1,0,2:T(8,128)S(1)} %copy.189), channel_id=1, source_target_pairs={{0,8},{8,16},{16,24},{24,32},{32,40},{40,48},{48,56},{56,64},{64,7... | collective-permute-start | bytes 98312 | tf_op jit(solution)/shard_map/ppermute | solution.py:44
  289.4 99.5 %collective-permute-start.5 = (f32[16,128,4]{1,0,2:T(8,128)S(1)}, f32[16,128,4]{1,0,2:T(8,128)S(1)}, u32[]{:S(2)}, u32[]{:S(2)}) collective-permute-start(f32[16,128,4]{1,0,2:T(8,128)S(1)} %copy.190), channel_id=1, source_target_pairs={{8,0},{16,8},{24,16},{32,24},{40,32},{48,40},{56,48},{64,56},{72,6... | collective-permute-start | bytes 98312 | tf_op jit(solution)/shard_map/ppermute | solution.py:46
  311.6 96.9 %collective-permute-start = (f32[16,128,4]{1,0,2:T(8,128)S(1)}, f32[16,128,4]{1,0,2:T(8,128)S(1)}, u32[]{:S(2)}, u32[]{:S(2)}) collective-permute-start(f32[16,128,4]{1,0,2:T(8,128)S(1)} %copy.180), channel_id=1, source_target_pairs={{0,8},{8,16},{16,24},{24,32},{32,40},{40,48},{48,56},{56,64},{64,7... | collective-permute-start | bytes 98312 | tf_op jit(solution)/shard_map/ppermute | solution.py:44
  316.6 94.6 %collective-permute-start.1 = (f32[16,128,4]{1,0,2:T(8,128)S(1)}, f32[16,128,4]{1,0,2:T(8,128)S(1)}, u32[]{:S(2)}, u32[]{:S(2)}) collective-permute-start(f32[16,128,4]{1,0,2:T(8,128)S(1)} %copy.181), channel_id=1, source_target_pairs={{8,0},{16,8},{24,16},{32,24},{40,32},{48,40},{56,48},{64,56},{72,6... | collective-permute-start | bytes 98312 | tf_op jit(solution)/shard_map/ppermute | solution.py:46
  338.9 109.2 %collective-permute-start.8 = (f32[16,128,4]{1,0,2:T(8,128)S(1)}, f32[16,128,4]{1,0,2:T(8,128)S(1)}, u32[]{:S(2)}, u32[]{:S(2)}) collective-permute-start(f32[16,128,4]{1,0,2:T(8,128)S(1)} %copy.198), channel_id=1, source_target_pairs={{0,8},{8,16},{16,24},{24,32},{32,40},{40,48},{48,56},{56,64},{64,7... | collective-permute-start | bytes 98312 | tf_op jit(solution)/shard_map/ppermute | solution.py:44
  396.4 20.8 %collective-permute-start.6 = (f32[16,4,128]{2,1,0:T(4,128)}, f32[16,4,128]{2,1,0:T(4,128)S(1)}, u32[]{:S(2)}, u32[]{:S(2)}) collective-permute-start(f32[16,4,128]{2,1,0:T(4,128)} %get-tuple-element.17), channel_id=1, source_target_pairs={{0,1},{1,2},{2,3},{3,4},{4,5},{5,6},{6,7},{8,9},{9,10},{10,11},{11... | collective-permute-start | bytes 98312 | tf_op jit(solution)/shard_map/ppermute | solution.py:44
  398.3 20.6 %collective-permute-start.7 = (f32[16,4,128]{2,1,0:T(4,128)}, f32[16,4,128]{2,1,0:T(4,128)S(1)}, u32[]{:S(2)}, u32[]{:S(2)}) collective-permute-start(f32[16,4,128]{2,1,0:T(4,128)} %get-tuple-element.18), channel_id=1, source_target_pairs={{1,0},{2,1},{3,2},{4,3},{5,4},{6,5},{7,6},{9,8},{10,9},{11,10},{12... | collective-permute-start | bytes 98312 | tf_op jit(solution)/shard_map/ppermute | solution.py:46
  408.5 44.9 %collective-permute-start.9 = (f32[16,128,4]{1,0,2:T(8,128)}, f32[16,128,4]{1,0,2:T(8,128)S(1)}, u32[]{:S(2)}, u32[]{:S(2)}) collective-permute-start(f32[16,128,4]{1,0,2:T(8,128)} %copy.199), channel_id=1, source_target_pairs={{8,0},{16,8},{24,16},{32,24},{40,32},{48,40},{56,48},{64,56},{72,6... | collective-permute-start | bytes 98312 | tf_op jit(solution)/shard_map/ppermute | solution.py:46
  411.2 78.4 %collective-permute-start.12 = (f32[16,128,4]{1,0,2:T(8,128)S(1)}, f32[16,128,4]{1,0,2:T(8,128)S(1)}, u32[]{:S(2)}, u32[]{:S(2)}) collective-permute-start(f32[16,128,4]{1,0,2:T(8,128)S(1)} %copy.207), channel_id=1, source_target_pairs={{0,8},{8,16},{16,24},{24,32},{32,40},{40,48},{48,56},{56,64},{64,7... | collective-permute-start | bytes 98312 | tf_op jit(solution)/shard_map/ppermute | solution.py:44
  417.2 75.4 %collective-permute-start.13 = (f32[16,128,4]{1,0,2:T(8,128)S(1)}, f32[16,128,4]{1,0,2:T(8,128)S(1)}, u32[]{:S(2)}, u32[]{:S(2)}) collective-permute-start(f32[16,128,4]{1,0,2:T(8,128)S(1)} %copy.208), channel_id=1, source_target_pairs={{8,0},{16,8},{24,16},{32,24},{40,32},{48,40},{56,48},{64,56},{72,6... | collective-permute-start | bytes 98312 | tf_op jit(solution)/shard_map/ppermute | solution.py:46
  424.5 38.6 %all-to-all-start.4 = ((f32[16,128,128]{1,2,0:T(8,128)}), f32[16,128,128]{1,2,0:T(8,128)}, u32[]{:S(2)}, u32[]{:S(2)}) async-start(f32[16,128,128]{1,2,0:T(8,128)} %convolution_bitcast_fusion.3), calls=%async_computation.4 | async-start | bytes 2097152 | tf_op jit(solution)/shard_map/all_to_all | solution.py:88
  463.1 35.2 %all-to-all-start.2 = ((f32[16,128,128]{1,2,0:T(8,128)}), f32[16,128,128]{1,2,0:T(8,128)}, u32[]{:S(2)}, u32[]{:S(2)}) async-start(f32[16,128,128]{1,2,0:T(8,128)} %convolution_bitcast_fusion.4), calls=%async_computation.2 | async-start | bytes 2097152 | tf_op jit(solution)/shard_map/all_to_all | solution.py:88
  475.3 18.6 %collective-permute-start.10 = (f32[16,4,128]{2,1,0:T(4,128)}, f32[16,4,128]{2,1,0:T(4,128)S(1)}, u32[]{:S(2)}, u32[]{:S(2)}) collective-permute-start(f32[16,4,128]{2,1,0:T(4,128)} %get-tuple-element.13), channel_id=1, source_target_pairs={{0,1},{1,2},{2,3},{3,4},{4,5},{5,6},{6,7},{8,9},{9,10},{10,11},{11... | collective-permute-start | bytes 98312 | tf_op jit(solution)/shard_map/ppermute | solution.py:44
  484.2 33.3 %collective-permute-start.16 = (f32[16,128,4]{1,0,2:T(8,128)S(1)}, f32[16,128,4]{1,0,2:T(8,128)S(1)}, u32[]{:S(2)}, u32[]{:S(2)}) collective-permute-start(f32[16,128,4]{1,0,2:T(8,128)S(1)} %copy.216), channel_id=1, source_target_pairs={{0,8},{8,16},{16,24},{24,32},{32,40},{40,48},{48,56},{56,64},{64,7... | collective-permute-start | bytes 98312 | tf_op jit(solution)/shard_map/ppermute | solution.py:44
  489.6 28.5 %collective-permute-start.17 = (f32[16,128,4]{1,0,2:T(8,128)S(1)}, f32[16,128,4]{1,0,2:T(8,128)S(1)}, u32[]{:S(2)}, u32[]{:S(2)}) collective-permute-start(f32[16,128,4]{1,0,2:T(8,128)S(1)} %copy.217), channel_id=1, source_target_pairs={{8,0},{16,8},{24,16},{32,24},{40,32},{48,40},{56,48},{64,56},{72,6... | collective-permute-start | bytes 98312 | tf_op jit(solution)/shard_map/ppermute | solution.py:46
  498.4 25.6 %all-to-all-start.6 = ((f32[16,128,128]{1,2,0:T(8,128)}), f32[16,128,128]{1,2,0:T(8,128)}, u32[]{:S(2)}, u32[]{:S(2)}) async-start(f32[16,128,128]{1,2,0:T(8,128)} %convolution_bitcast_fusion.2), calls=%async_computation.6 | async-start | bytes 2097152 | tf_op jit(solution)/shard_map/all_to_all | solution.py:88
  523.9 26.2 %all-to-all-start.8 = ((f32[16,128,128]{1,2,0:T(8,128)}), f32[16,128,128]{1,2,0:T(8,128)S(1)}, u32[]{:S(2)}, u32[]{:S(2)}) async-start(f32[16,128,128]{1,2,0:T(8,128)} %convolution_bitcast_fusion.1), calls=%async_computation.8 | async-start | bytes 2097152 | tf_op jit(solution)/shard_map/all_to_all | solution.py:88
  550.2 25.1 %all-to-all-start.10 = ((f32[16,128,128]{1,2,0:T(8,128)}), f32[16,128,128]{1,2,0:T(8,128)S(1)}, u32[]{:S(2)}, u32[]{:S(2)}) async-start(f32[16,128,128]{1,2,0:T(8,128)} %convolution_bitcast_fusion), calls=%async_computation.10 | async-start | bytes 2097152 | tf_op jit(solution)/shard_map/all_to_all | solution.py:88
  (17 other events, 123.4 us)
